TPU v7x, 32 devices: a whole 2x2x4 slice. The times are simulated.
32 devices in a mesh: req: 4 (over y, x), exp: 8 (over z, core).
Axes of the slice: x: 2, y: 2, z: 4, core: 2. Of those that a mesh axis runs over, the one named last changes fastest.
Arguments:
- tokens: bfloat16 [4, 512, 2048], P('req', 'exp'), may hold values from -6 to 6
- cache: bfloat16 [4, 1024, 4096], P('req', None, 'exp'), may hold values from -64 to 64
- cache_len: int32 [4], P('req'), may hold values from 1 to 1024, 2560 in all
- attn_routes: int32 [4, 512, 2], P('req', 'exp'), may hold values from 0 to 7, all different within a row; in each aligned block of 64 rows (0 to 63, 64 to 127, ..., all dimensions but the last counted through in order) at most 24 rows name the same one
- mlp_routes: int32 [4, 512, 2], P('req', 'exp'), may hold values from 0 to 7, all different within a row; in each aligned block of 64 rows (0 to 63, 64 to 127, ..., all dimensions but the last counted through in order) at most 24 rows name the same one
- norm_attn: float32 [2048], replicated, may hold values from 0.5 to 1.5
- attn_router: bfloat16 [2048, 8], replicated, may hold values from -0.125 to 0.125
- w_query: bfloat16 [128, 2048, 128], P('exp'), may hold values from -0.125 to 0.125
- w_keyval: bfloat16 [2048, 4096], P(None, 'exp'), may hold values from -0.125 to 0.125
- w_out: bfloat16 [128, 128, 2048], P('exp'), may hold values from -0.125 to 0.125
- norm_mlp: float32 [2048], replicated, may hold values from 0.5 to 1.5
- mlp_router: bfloat16 [2048, 8], replicated, may hold values from -0.125 to 0.125
- w_gate: bfloat16 [8, 2048, 5632], P('exp'), may hold values from -0.125 to 0.125
- w_up: bfloat16 [8, 2048, 5632], P('exp'), may hold values from -0.125 to 0.125
- w_down: bfloat16 [8, 5632, 2048], P('exp'), may hold values from -0.078125 to 0.078125
Outputs:
- hidden_out: bfloat16 [4, 512, 2048], P('req', 'exp')
- cache_out: bfloat16 [4, 1536, 4096], P('req', None, 'exp')
Inputs may be any that keep to these rules, and one draw needn't show every extreme that they name: `attn_routes`: in each aligned block of 64 rows, no expert is named by more than 24 rows. `mlp_routes`: in each aligned block of 64 rows, no expert is named by more than 24 rows.
All inputs are finite; a program needn't handle non-finite values. No bound on the sum of `cache_len` on one device may be relied on, other than what follows from the above.
Results may differ from a plain program's by a relative error of at most 0.015.
The roundings to bfloat16 on the way count: a program that leaves them out, or rounds other values in their place, can miss the bound.
Values may be sent and summed in bfloat16 or wider, within the bound.
No kernel may reach another device: no remote copies, remote signals or barrier semaphores. Data moves between devices by JAX's collectives and lax.ppermute only.
A program may use at most 256 MiB of HBM per device.

v0:
```python
import math
import jax
import jax.numpy as jnp
from jax import lax
from jax.sharding import PartitionSpec as P

MOST = 24
epsilon = 1e-05
rope_base = 10000.0
masked_score = -1e30


def from_partner(value, axis, stride):
    mask = 2**stride
    pairs = [(source, source ^ mask) for source in range(lax.axis_size(axis))]
    return lax.ppermute(value, axis, pairs)


def rms_norm(values, gain_vec):
    widened = values.astype(jnp.float32)
    inv_rms = lax.rsqrt(jnp.mean(widened * widened, axis=-1, keepdims=True) + epsilon)
    return (widened * inv_rms * gain_vec).astype(jnp.bfloat16)


def rotate(values, position):
    half_dim = values.shape[-1] // 2
    inv_freq = rope_base ** (-jnp.arange(half_dim).astype(jnp.float32) / half_dim)
    angles = position.astype(jnp.float32)[..., None] * inv_freq
    cosine = jnp.cos(angles)
    sines = jnp.sin(angles)
    first_half = values[..., :half_dim]
    second_half = values[..., half_dim:]
    return jnp.concatenate(
        [first_half * cosine - second_half * sines, second_half * cosine + first_half * sines],
        axis=-1,
    )


def pick_gates(normed, router, routes):
    logits = jnp.dot(normed, router, preferred_element_type=jnp.float32)
    labels = jnp.arange(router.shape[1], dtype=jnp.int32)
    onehot = (routes[:, :, None] == labels[None, None, :]).astype(jnp.float32)
    chosen = jnp.sum(onehot * logits[:, None, :], axis=-1)
    return jax.nn.softmax(chosen, axis=-1)


def slot_tables(routes, gates, labels, rows_block, slot_count):
    row_total = routes.shape[0]
    block_count = row_total // rows_block
    matches = routes[:, :, None] == labels[None, None, :]
    member = jnp.any(matches, axis=1).astype(jnp.int32).reshape(block_count, rows_block, -1)
    weight = jnp.sum(jnp.where(matches, gates[:, :, None], 0.0), axis=1).reshape(
        block_count, rows_block, -1
    )
    ranking = jnp.cumsum(member, axis=1) - 1
    slot_ids = jnp.arange(slot_count, dtype=jnp.int32)
    onehot = ((member[..., None] > 0) & (ranking[..., None] == slot_ids)).astype(jnp.int32)
    local_row = jnp.arange(rows_block, dtype=jnp.int32)[None, :, None, None]
    token_ids = (
        jnp.sum(onehot * local_row, axis=1)
        + (jnp.arange(block_count, dtype=jnp.int32) * rows_block)[:, None, None]
    )
    shares = jnp.sum(onehot.astype(jnp.float32) * weight[..., None], axis=1)
    return (token_ids, shares)


def spread_rows(terms, token_ids, extent):
    term_part = terms.reshape(-1, terms.shape[-1])
    id_part = token_ids.reshape(-1)
    return jnp.zeros((extent, terms.shape[-1]), jnp.float32).at[id_part].add(term_part, mode="drop")


def attend(queries, query_pos, key_cache, value_cache, key_fresh, value_fresh, length):
    query_count = queries.shape[0]
    head_dim = queries.shape[1]
    factor = head_dim ** (-0.5)

    def absorb(state, key_block, value_block, visible):
        running_top, running_total, running_acc = state
        scores = jnp.dot(queries, key_block.T, preferred_element_type=jnp.float32) * factor
        scores = jnp.where(visible, scores, masked_score)
        new_top = jnp.maximum(running_top, jnp.max(scores, axis=1))
        fading = jnp.exp(running_top - new_top)
        weights = jnp.exp(scores - new_top[:, None])
        running_total = running_total * fading + jnp.sum(weights, axis=1)
        running_acc = running_acc * fading[:, None] + jnp.dot(
            weights.astype(jnp.bfloat16), value_block, preferred_element_type=jnp.float32
        )
        return (new_top, running_total, running_acc)

    state = (
        jnp.full((query_count,), masked_score, jnp.float32),
        jnp.zeros((query_count,), jnp.float32),
        jnp.zeros((query_count, head_dim), jnp.float32),
    )
    cache_span = math.gcd(512, key_cache.shape[0])

    def cache_step(step_idx, state):
        offset = step_idx * cache_span
        key_block = lax.dynamic_slice_in_dim(key_cache, offset, cache_span, 0)
        value_block = lax.dynamic_slice_in_dim(value_cache, offset, cache_span, 0)
        visible = (offset + jnp.arange(cache_span, dtype=jnp.int32))[None, :] < length
        return absorb(state, key_block, value_block, visible)

    state = lax.fori_loop(0, (length + cache_span - 1) // cache_span, cache_step, state)
    fresh_span = math.gcd(512, key_fresh.shape[0])
    for offset in range(0, key_fresh.shape[0], fresh_span):
        visible = (offset + jnp.arange(fresh_span, dtype=jnp.int32))[None, :] <= query_pos[:, None]
        state = absorb(
            state,
            key_fresh[offset : offset + fresh_span],
            value_fresh[offset : offset + fresh_span],
            visible,
        )
    running_top, running_total, running_acc = state
    return (running_acc / running_total[:, None]).astype(jnp.bfloat16)


def body(
    tokens,
    cache,
    cache_len,
    attn_routes,
    mlp_routes,
    norm_attn,
    attn_router,
    w_query,
    w_keyval,
    w_out,
    norm_mlp,
    mlp_router,
    w_gate,
    w_up,
    w_down,
):
    device_count = lax.axis_size("exp")
    position = lax.axis_index("exp")
    own_rows = tokens[0]
    rows_block = own_rows.shape[0]
    model_width = own_rows.shape[1]
    length = cache_len[0]
    slot_count = MOST
    normed = rms_norm(own_rows, norm_attn)
    group_normed, group_routes = (
        lax.all_gather(normed, "exp", axis=0, tiled=True),
        lax.all_gather(attn_routes[0], "exp", axis=0, tiled=True),
    )
    row_total = group_normed.shape[0]
    block_count = row_total // rows_block
    heads_here = w_query.shape[0]
    head_dim = w_query.shape[2]
    columns = w_keyval.shape[1]
    experts_attn = attn_router.shape[1]
    my_attn = jnp.reshape(position % experts_attn, (1,))
    new_pos = length + jnp.arange(row_total, dtype=jnp.int32)
    fresh_kv = jnp.dot(group_normed, w_keyval, preferred_element_type=jnp.float32)
    if columns < 2 * head_dim:
        is_key = position % 2 == 0
        fresh_kv = jnp.where(is_key, rotate(fresh_kv, new_pos), fresh_kv).astype(jnp.bfloat16)
    else:
        split_new = fresh_kv.reshape(row_total, columns // (2 * head_dim), 2, head_dim)
        rotated = rotate(split_new[:, :, 0], new_pos[:, None])
        fresh_kv = (
            jnp.stack([rotated, split_new[:, :, 1]], axis=2)
            .astype(jnp.bfloat16)
            .reshape(row_total, columns)
        )
    cache_limit = cache.shape[1]
    padded = jnp.concatenate([cache[0], jnp.zeros((row_total, columns), jnp.bfloat16)], axis=0)
    placed = lax.dynamic_update_slice(jnp.zeros_like(padded), fresh_kv, (length, jnp.int32(0)))
    slot_ids = jnp.arange(cache_limit + row_total, dtype=jnp.int32)
    cache_next = jnp.where((slot_ids < length)[:, None], padded, placed)
    group_cache = cache[0]
    group_fresh = fresh_kv
    for bit in range(experts_attn.bit_length() - 1):
        other_cache, other_fresh = from_partner((group_cache, group_fresh), "exp", bit)
        lower = position // (1 << bit) % 2 == 0
        group_cache = jnp.where(
            lower,
            jnp.concatenate([group_cache, other_cache], axis=1),
            jnp.concatenate([other_cache, group_cache], axis=1),
        )
        group_fresh = jnp.where(
            lower,
            jnp.concatenate([group_fresh, other_fresh], axis=1),
            jnp.concatenate([other_fresh, group_fresh], axis=1),
        )
    split_old = group_cache.reshape(cache_limit, heads_here, 2, head_dim)
    split_fresh = group_fresh.reshape(row_total, heads_here, 2, head_dim)
    attn_gates = pick_gates(group_normed, attn_router, group_routes)
    attn_tokens, attn_shares = slot_tables(
        group_routes, attn_gates, my_attn, rows_block, slot_count
    )
    token_flat = attn_tokens[:, 0, :].reshape(-1)
    share_flat = attn_shares[:, 0, :].reshape(-1)
    picked_rows = group_normed[token_flat]
    queries = jnp.einsum("sd,hdk->hsk", picked_rows, w_query, preferred_element_type=jnp.float32)
    queries = rotate(queries, (length + token_flat)[None, :]).astype(jnp.bfloat16)
    attend_heads = jax.vmap(attend, in_axes=(0, None, 1, 1, 1, 1, None))
    head_outs = attend_heads(
        queries,
        token_flat,
        split_old[:, :, 0],
        split_old[:, :, 1],
        split_fresh[:, :, 0],
        split_fresh[:, :, 1],
        length,
    )
    projected = jnp.einsum("hsk,hkd->sd", head_outs, w_out, preferred_element_type=jnp.float32)
    projected = (projected * share_flat[:, None]).reshape(block_count, slot_count, model_width)
    attn_ids = attn_tokens[:, 0, :]
    attn_own = lax.psum_scatter(
        spread_rows(projected, attn_ids, rows_block * lax.axis_size("exp")).astype(jnp.bfloat16),
        "exp",
        scatter_dimension=0,
        tiled=True,
    ).astype(jnp.float32)
    middle = lax.optimization_barrier(
        (own_rows.astype(jnp.float32) + attn_own).astype(jnp.bfloat16)
    )
    normed_mlp = rms_norm(middle, norm_mlp)
    experts_mlp = mlp_router.shape[1]
    split_count = device_count // experts_mlp
    my_expert = jnp.reshape(position // split_count, (1,))
    all_normed, all_routes = (
        lax.all_gather(normed_mlp, "exp", axis=0, tiled=True),
        lax.all_gather(mlp_routes[0], "exp", axis=0, tiled=True),
    )
    all_gates = pick_gates(all_normed, mlp_router, all_routes)
    mlp_tokens, mlp_shares = slot_tables(all_routes, all_gates, my_expert, rows_block, slot_count)
    inputs = all_normed[mlp_tokens.reshape(-1)]
    gate_part = jnp.dot(inputs, w_gate[0], preferred_element_type=jnp.float32)
    up_part = jnp.dot(inputs, w_up[0], preferred_element_type=jnp.float32)
    hidden = (jax.nn.silu(gate_part) * up_part).astype(jnp.bfloat16)
    slice_out = lax.optimization_barrier(
        jnp.dot(hidden, w_down[0], preferred_element_type=jnp.float32).astype(jnp.bfloat16)
    )
    weighted = (slice_out.astype(jnp.float32) * mlp_shares.reshape(-1)[:, None]).reshape(
        block_count, slot_count, model_width
    )
    mlp_ids = mlp_tokens[:, 0, :]
    mlp_own = lax.psum_scatter(
        spread_rows(weighted, mlp_ids, rows_block * lax.axis_size("exp")).astype(jnp.bfloat16),
        "exp",
        scatter_dimension=0,
        tiled=True,
    ).astype(jnp.float32)
    layer_out = (middle.astype(jnp.float32) + mlp_own).astype(jnp.bfloat16)
    return (layer_out[None], cache_next[None])


def solution(mesh):
    placed = (
        P("req", "exp", None),
        P("req", None, "exp"),
        P("req"),
        P("req", "exp", None),
        P("req", "exp", None),
        P(),
        P(),
        P("exp", None, None),
        P(None, "exp"),
        P("exp", None, None),
        P(),
        P(),
        P("exp", None, None),
        P("exp", None, None),
        P("exp", None, None),
    )
    return jax.shard_map(
        body,
        mesh=mesh,
        in_specs=placed,
        out_specs=(P("req", "exp", None), P("req", None, "exp")),
        check_vma=False,
    )
```

profile of v0, /device:TPU:0, one launch (start us, length us, event | category | flops | bytes accessed | tf_op | source)
XLA Modules:
  0.0 598.1 jit_solution(17848477500451785109)
XLA Ops:
  14.5 16.4 %all-gather = s32[1,512,2]{2,0,1:T(1,128)S(1)} all-gather(s32[1,64,2]{2,0,1:T(1,128)S(1)} %copy.70), channel_id=2, replica_groups=mesh['req'=4,'exp'=8] {'exp'}, dimensions={1}, use_global_device_ids=true | all-gather | bytes 4608 | tf_op jit(solution)/shard_map/all_gather | solution.py:146
  31.8 15.1 %all-gather.1 = s32[1,512,2]{2,0,1:T(1,128)S(1)} all-gather(s32[1,64,2]{2,0,1:T(1,128)S(1)} %copy.88), channel_id=3, replica_groups=mesh['req'=4,'exp'=8] {'exp'}, dimensions={1}, use_global_device_ids=true | all-gather | bytes 4608 | tf_op jit(solution)/shard_map/all_gather | solution.py:227
  61.1 38.7 %collective-permute-done.1 = bf16[1024,1024]{1,0:T(8,128)(2,1)} collective-permute-done((bf16[1024,1024]{1,0:T(8,128)(2,1)}, bf16[1024,1024]{1,0:T(8,128)(2,1)}, u32[]{:S(2)}, u32[]{:S(2)}) %collective-permute-start.1) | collective-permute-done | bytes 2097184 | tf_op jit(solution)/shard_map/ppermute | solution.py:16
  99.8 6.7 %maximum_select_fusion.2 = bf16[1024,2048]{1,0:T(8,128)(2,1)} fusion(bf16[1024,1024]{1,0:T(8,128)(2,1)} %collective-permute-done.1, bf16[1024,1024]{1,0:T(8,128)(2,1)} %maximum_select_fusion.5, pred[]{:T(512)S(6)} %eq.114), kind=kLoop, calls=%fused_computation.44 | loop fusion | flops 18874368 | bytes 8388609 | tf_op jit(solution)/shard_map/jit(_where)/select_n | solution.py:178
  112.9 5.1 maximum_select_fusion.1
  129.1 5.4 convolution_bitcast_fusion.1
  137.1 84.4 %collective-permute-done.4 = bf16[512,1024]{0,1:T(8,128)(2,1)S(1)} collective-permute-done((bf16[512,1024]{0,1:T(8,128)(2,1)S(1)}, bf16[512,1024]{0,1:T(8,128)(2,1)S(1)}, u32[]{:S(2)}, u32[]{:S(2)}) %collective-permute-start.4) | collective-permute-done | bytes 1048608 | tf_op jit(solution)/shard_map/ppermute | solution.py:16
  227.7 108.2 %collective-permute-done.2 = bf16[1024,2048]{1,0:T(8,128)(2,1)} collective-permute-done((bf16[1024,2048]{1,0:T(8,128)(2,1)}, bf16[1024,2048]{1,0:T(8,128)(2,1)}, u32[]{:S(2)}, u32[]{:S(2)}) %collective-permute-start.2) | collective-permute-done | bytes 4194336 | tf_op jit(solution)/shard_map/ppermute | solution.py:16
  335.9 6.4 %copy.75 = bf16[1024,2048]{0,1:T(8,128)(2,1)} copy(bf16[1024,2048]{1,0:T(8,128)(2,1)} %collective-permute-done.2) | data formatting | bytes 8388608 | tf_op jit(solution)/shard_map/ppermute | solution.py:16
  342.3 6.6 %maximum_select_fusion = bf16[1024,16,2,128]{0,3,2,1:T(8,128)(2,1)S(1)} fusion(bf16[1024,8,2,128]{0,3,2,1:T(8,128)(2,1)} %bitcast.160, bf16[1024,8,2,128]{0,3,2,1:T(8,128)(2,1)} %maximum_select_fusion.1, pred[]{:T(512)S(6)} %eq.113), kind=kLoop, calls=%fused_computation.33 | loop fusion | flops 12582912 | bytes 16777216 | tf_op jit(solution)/shard_map/jit(_where)/select_n | solution.py:178
  353.9 55.1 %while.16 = (s32[]{:T(128)}, f32[16,192]{1,0:T(8,128)S(1)}, f32[16,192]{1,0:T(8,128)S(1)}, f32[16,192,128]{2,1,0:T(8,128)}, s32[]{:T(128)}, /*index=5*/s32[]{:T(...) while((s32[]{:T(128)}, f32[16,192]{1,0:T(8,128)S(1)}, ...), condition=%wide.region_7.8_spmd, body=%wide.region_4.7_spmd.sunk | while | flops 823401472 | bytes 69142768 | solution.py:105
  354.7 6.4 %constant_dynamic-slice_fusion.3 = (bf16[512,16,128]{0,2,1:T(8,128)(2,1)S(1)}, bf16[512,16,128]{0,2,1:T(8,128)(2,1)}) fusion(bf16[1024,16,128]{0,2,1:T(8,128)(2,1)} %get-tuple-element.252, s32[]{:T(128)S(1)} %bitcast.175, bf16[1024,16,128]{0,2,1:T(8,128)(2,1)} %get-tuple-element.250), kind=kLoop, calls=%fused_computation.23.clone.1 | loop fusion | bytes 8388612 | tf_op jit(solution)/shard_map/vmap()/while
  374.6 6.9 %multiply_add_fusion.7 = f32[16,192,128]{2,1,0:T(8,128)} fusion(f32[16,192,128]{2,1,0:T(8,128)} %get-tuple-element.233, bf16[512,16,128]{2,0,1:T(8,128)(2,1)} %copy.105, f32[16,512,192]{1,2,0:T(8,128)} %copy-done.2, f32[16,192]{1,0:T(8,128)S(1)} %max.10, pred[512]{0:T(512)(128)(4,1)S(1)} %add_compare_fusion.2, f32[16,192]{1,0:T(8,128)S(1)} %get-tuple-element.215), kind=kOutput, calls=%fused_computation.18.clone.1 | convolution fusion | flops 409731072 | bytes 11559424 | tf_op jit(solution)/shard_map/vmap()/while/body/dot_general | solution.py:86
  382.3 6.1 %constant_dynamic-slice_fusion.3 = (bf16[512,16,128]{0,2,1:T(8,128)(2,1)S(1)}, bf16[512,16,128]{0,2,1:T(8,128)(2,1)}) fusion(bf16[1024,16,128]{0,2,1:T(8,128)(2,1)} %get-tuple-element.252, s32[]{:T(128)S(1)} %bitcast.175, bf16[1024,16,128]{0,2,1:T(8,128)(2,1)} %get-tuple-element.250), kind=kLoop, calls=%fused_computation.23.clone.1 | loop fusion | bytes 8388612 | tf_op jit(solution)/shard_map/vmap()/while
  402.0 6.9 %multiply_add_fusion.7 = f32[16,192,128]{2,1,0:T(8,128)} fusion(f32[16,192,128]{2,1,0:T(8,128)} %get-tuple-element.233, bf16[512,16,128]{2,0,1:T(8,128)(2,1)} %copy.105, f32[16,512,192]{1,2,0:T(8,128)} %copy-done.2, f32[16,192]{1,0:T(8,128)S(1)} %max.10, pred[512]{0:T(512)(128)(4,1)S(1)} %add_compare_fusion.2, f32[16,192]{1,0:T(8,128)S(1)} %get-tuple-element.215), kind=kOutput, calls=%fused_computation.18.clone.1 | convolution fusion | flops 409731072 | bytes 11559424 | tf_op jit(solution)/shard_map/vmap()/while/body/dot_general | solution.py:86
  409.1 4.3 maximum_select_fusion.3
  420.2 10.8 %fusion.39 = f32[192,2048]{1,0:T(8,128)} fusion(bf16[16,128,2048]{2,1,0:T(8,128)(2,1)} %param.26, f32[16,192,128]{2,1,0:T(8,128)S(1)} %copy-done.11, bf16[512,16,2,128]{0,3,1,2:T(8,128)(2,1)} %copy-done.8, f32[16,192,512]{2,1,0:T(8,128)} %copy-done.5, f32[16,192]{1,0:T(8,128)S(1)} %max.8, pred[192,512]{1,0:T(8,128)(4,1)S(1)} %iota_compare_fusion, ...), kind=kOutput, calls=%fused_computation.52 | convolution fusion | flops 2021523456 | bytes 20058880 | tf_op jit(solution)/shard_map/hsk,hkd->sd/dot_general | solution.py:209
  431.0 5.9 scatter_custom_fusion
  440.9 36.0 %reduce-scatter.3.cloned.1.call-done = bf16[64,2048]{1,0:T(8,128)(2,1)} async-done(((bf16[512,2048]{1,0:T(8,128)(2,1)}), bf16[64,2048]{1,0:T(8,128)(2,1)}) %reduce-scatter.3.cloned.1.call-update) | async-done | bytes 262160 | tf_op jit(solution)/shard_map/reduce_scatter | solution.py:212
  479.2 27.5 %all-gather.7.cloned.1.call-done = bf16[512,2048]{1,0:T(8,128)(2,1)} async-done(((bf16[64,2048]{1,0:T(8,128)(2,1)}), bf16[512,2048]{1,0:T(8,128)(2,1)}) %all-gather.7.cloned.1.call-update) | async-done | bytes 2097168 | tf_op jit(solution)/shard_map/all_gather | solution.py:226
  511.4 12.0 %fusion.22 = f32[192,5632]{1,0:T(8,128)} fusion(bf16[192,2048]{1,0:T(8,128)(2,1)S(1)} %gather_fusion.1, bf16[1,2048,5632]{2,1,0:T(8,128)(2,1)} %param.29), kind=kOutput, calls=%fused_computation.31 | convolution fusion | flops 4429185024 | bytes 28180480 | tf_op jit(solution)/shard_map/dot_general | solution.py:232
  523.4 20.6 %fusion.40 = bf16[192,2048]{1,0:T(8,128)(2,1)S(1)} fusion(bf16[1,5632,2048]{2,1,0:T(8,128)(2,1)} %param.31, bf16[192,2048]{1,0:T(8,128)(2,1)} %copy-done.12, bf16[1,2048,5632]{2,1,0:T(8,128)(2,1)} %param.30, f32[192,5632]{1,0:T(8,128)} %fusion.22), kind=kOutput, calls=%fused_computation.53 | convolution fusion | flops 8865251328 | bytes 52035584 | tf_op jit(solution)/shard_map/dot_general | solution.py:236
  545.1 5.2 scatter_custom_fusion.1
  564.8 24.8 %reduce-scatter.5.cloned.1.call-done = bf16[64,2048]{1,0:T(8,128)(2,1)} async-done(((bf16[512,2048]{1,0:T(8,128)(2,1)}), bf16[64,2048]{1,0:T(8,128)(2,1)}) %reduce-scatter.5.cloned.1.call-update) | async-done | bytes 262160 | tf_op jit(solution)/shard_map/reduce_scatter | solution.py:242
  (178 shorter events, 116.2 us)
Async XLA Ops:
  7.2 110.8 %copy-start = (bf16[2048,512]{1,0:T(8,128)(2,1)S(1)}, bf16[2048,512]{1,0:T(8,128)(2,1)}, u32[]{:S(2)}) copy-start(bf16[2048,512]{1,0:T(8,128)(2,1)} %param.25) | copy-start | bytes 6291460
  7.2 40.8 %copy-start.6 = (bf16[1,1024,512]{2,1,0:T(8,128)(2,1)S(1)}, bf16[1,1024,512]{2,1,0:T(8,128)(2,1)}, u32[]{:S(2)}) copy-start(bf16[1,1024,512]{2,1,0:T(8,128)(2,1)} %param.18) | copy-start | bytes 3145732
  7.2 110.8 %all-gather.5.cloned.1.call-start = ((), (), s32[]{:S(2)}) async-start(), calls=%async_computation.2 | async-start | bytes 2359296 | tf_op jit(solution)/shard_map/all_gather | solution.py:145
  7.2 40.8 %collective-permute-start = (bf16[1024,512]{1,0:T(8,128)(2,1)}, bf16[1024,512]{1,0:T(8,128)(2,1)}, u32[]{:S(2)}, u32[]{:S(2)}) collective-permute-start(bf16[1024,512]{1,0:T(8,128)(2,1)} %bitcast.161), channel_id=1, source_target_pairs={{0,1},{1,0},{2,3},{3,2},{4,5},{5,4},{6,7},{7,6},{8,9},{9,8},{10,11... | collective-permute-start | bytes 3145736 | tf_op jit(solution)/shard_map/ppermute | solution.py:16
  10.7 466.2 %reduce-scatter.3.cloned.1.call-start = ((), (), s32[]{:S(2)}) async-start(), calls=%async_computation.3 | async-start | bytes 2359296 | tf_op jit(solution)/shard_map/reduce_scatter | solution.py:212
  46.9 7.0 %copy-start.15 = (s32[1,512,2]{1,2,0:T(2,128)}, s32[1,512,2]{1,2,0:T(2,128)S(1)}, u32[]{:S(2)}) copy-start(s32[1,512,2]{1,2,0:T(2,128)S(1)} %copy.89) | copy-start | bytes 12292
  51.6 48.2 %collective-permute-start.1 = (bf16[1024,1024]{1,0:T(8,128)(2,1)}, bf16[1024,1024]{1,0:T(8,128)(2,1)}, u32[]{:S(2)}, u32[]{:S(2)}) collective-permute-start(bf16[1024,1024]{1,0:T(8,128)(2,1)} %maximum_select_fusion.5), channel_id=1, source_target_pairs={{0,2},{1,3},{2,0},{3,1},{4,6},{5,7},{6,4},{7,5},{8,10},{9,11},{10,... | collective-permute-start | bytes 6291464 | tf_op jit(solution)/shard_map/ppermute | solution.py:16
  106.5 229.4 %collective-permute-start.2 = (bf16[1024,2048]{1,0:T(8,128)(2,1)}, bf16[1024,2048]{1,0:T(8,128)(2,1)}, u32[]{:S(2)}, u32[]{:S(2)}) collective-permute-start(bf16[1024,2048]{1,0:T(8,128)(2,1)} %maximum_select_fusion.2), channel_id=1, source_target_pairs={{0,4},{1,5},{2,6},{3,7},{4,0},{5,1},{6,2},{7,3},{8,12},{9,13},{10,... | collective-permute-start | bytes 12582920 | tf_op jit(solution)/shard_map/ppermute | solution.py:16
  121.2 4.5 collective-permute-start.3
  127.3 7.3 %copy-start.13 = (f32[192,64]{1,0:T(8,128)S(1)}, f32[192,64]{1,0:T(8,128)}, u32[]{:S(2)}) copy-start(f32[192,64]{1,0:T(8,128)} %get-tuple-element.140) | copy-start | bytes 147460
  127.3 7.3 %copy-start.14 = (f32[192,64]{1,0:T(8,128)S(1)}, f32[192,64]{1,0:T(8,128)}, u32[]{:S(2)}) copy-start(f32[192,64]{1,0:T(8,128)} %get-tuple-element.141) | copy-start | bytes 147460
  127.3 94.2 %collective-permute-start.4 = (bf16[512,1024]{0,1:T(8,128)(2,1)S(1)}, bf16[512,1024]{0,1:T(8,128)(2,1)S(1)}, u32[]{:S(2)}, u32[]{:S(2)}) collective-permute-start(bf16[512,1024]{0,1:T(8,128)(2,1)S(1)} %maximum_select_fusion.9), channel_id=1, source_target_pairs={{0,2},{1,3},{2,0},{3,1},{4,6},{5,7},{6,4},{7,5},{8,10},{9,11},{10,... | collective-permute-start | bytes 3145736 | tf_op jit(solution)/shard_map/ppermute | solution.py:16
  223.5 185.5 %collective-permute-start.5 = (bf16[512,2048]{0,1:T(8,128)(2,1)}, bf16[512,2048]{0,1:T(8,128)(2,1)}, u32[]{:S(2)}, u32[]{:S(2)}) collective-permute-start(bf16[512,2048]{0,1:T(8,128)(2,1)} %maximum_select_fusion.7), channel_id=1, source_target_pairs={{0,4},{1,5},{2,6},{3,7},{4,0},{5,1},{6,2},{7,3},{8,12},{9,13},{10,... | collective-permute-start | bytes 6291464 | tf_op jit(solution)/shard_map/ppermute | solution.py:16
  437.0 40.0 %copy-start.10 = (bf16[1,64,2048]{2,1,0:T(8,128)(2,1)S(1)}, bf16[1,64,2048]{2,1,0:T(8,128)(2,1)}, u32[]{:S(2)}) copy-start(bf16[1,64,2048]{2,1,0:T(8,128)(2,1)} %param.17) | copy-start | bytes 786436
  437.0 41.1 %copy-start.23 = (f32[2048]{0:T(1024)S(1)}, f32[2048]{0:T(1024)}, u32[]{:S(2)}) copy-start(f32[2048]{0:T(1024)} %param.27) | copy-start | bytes 24580
  440.9 65.9 %all-gather.7.cloned.1.call-start = ((), (), s32[]{:S(2)}) async-start(), calls=%async_computation.4 | async-start | bytes 2359296 | tf_op jit(solution)/shard_map/all_gather | solution.py:226
  479.0 110.6 %reduce-scatter.5.cloned.1.call-start = ((), (), s32[]{:S(2)}) async-start(), calls=%async_computation.5 | async-start | bytes 2359296 | tf_op jit(solution)/shard_map/reduce_scatter | solution.py:242
  523.3 20.7 %copy-start.4 = (bf16[512,2048]{1,0:T(8,128)(2,1)S(1)}, bf16[512,2048]{1,0:T(8,128)(2,1)}, u32[]{:S(2)}) copy-start(bf16[512,2048]{1,0:T(8,128)(2,1)} %all-gather.7.cloned.1.call-done) | copy-start | bytes 6291460
  523.3 20.7 %copy-start.20 = (bf16[2048,8]{0,1:T(8,128)(2,1)S(1)}, bf16[2048,8]{0,1:T(8,128)(2,1)}, u32[]{:S(2)}) copy-start(bf16[2048,8]{0,1:T(8,128)(2,1)} %param.28) | copy-start | bytes 98308
  523.4 21.3 %copy-start.16 = (s32[1,512,2]{1,2,0:T(2,128)S(1)}, s32[1,512,2]{1,2,0:T(2,128)}, u32[]{:S(2)}) copy-start(s32[1,512,2]{1,2,0:T(2,128)} %copy-done.15) | copy-start | bytes 12292
  523.4 21.5 %copy-start.18 = (s32[8,64]{1,0:T(8,128)S(1)}, s32[8,64]{1,0:T(8,128)}, u32[]{:S(2)}) copy-start(s32[8,64]{1,0:T(8,128)} %copy-done.17) | copy-start | bytes 6148
  523.4 21.5 %copy-start.22 = (pred[8,64]{1,0:T(8,128)(4,1)S(1)}, pred[8,64]{1,0:T(8,128)(4,1)}, u32[]{:S(2)}) copy-start(pred[8,64]{1,0:T(8,128)(4,1)} %copy-done.21) | copy-start | bytes 1540
  554.1 7.6 %copy-start.7 = (bf16[1,1024,512]{2,1,0:T(8,128)(2,1)S(1)}, bf16[1,1024,512]{2,1,0:T(8,128)(2,1)}, u32[]{:S(2)}) copy-start(bf16[1,1024,512]{2,1,0:T(8,128)(2,1)} %param.18) | copy-start | bytes 3145732
  554.2 37.1 %copy-start.1 = (bf16[2048,512]{1,0:T(8,128)(2,1)S(1)}, bf16[2048,512]{1,0:T(8,128)(2,1)}, u32[]{:S(2)}) copy-start(bf16[2048,512]{1,0:T(8,128)(2,1)} %param.25) | copy-start | bytes 6291460
  (11 other events, 30.4 us)
Sparse Core Ops, SparseCore 0:
  10.8 34.0 all-gather.4
  441.0 35.8 reduce-scatter.2
  479.1 27.5 all-gather.6
  554.3 35.2 reduce-scatter.4
where the time goes:
time: 603 us; the launch traced here: 598 us
  waiting for transfers between devices  320 us (53%)
  other arithmetic  76.5 us (13%)
  matrix products  73.7 us (12%)
  local copies, waits for them, and re-layouts  72 us (12%)
  blocking collectives  31.5 us (5%)
  between operations  15.2 us (3%)
  starting transfers between devices  9.33 us (2%)
    ppermute x6, waiting for transfers between devices, from_partner(): return lax.ppermute(value, axis, pairs)  231 us
    reduce_scatter x1, waiting for transfers between devices, body(): lax.psum_scatter(spread_rows(projected, attn_ids, rows_block * lax.axis_s...  36 us
    while x12, local copies, waits for them, and re-layouts  30.4 us
    all_gather x1, waiting for transfers between devices, body(): lax.all_gather(normed_mlp, 'exp', axis=0, tiled=True)  27.5 us
    select_n x5, other arithmetic, body(): jnp.where(lower, jnp.concatenate([group_cache, other_cache], axis=1), jnp...  25.2 us
    reduce_scatter x1, waiting for transfers between devices, body(): lax.psum_scatter(spread_rows(weighted, mlp_ids, rows_block * lax.axis_siz...  24.8 us
    dot_general x1, matrix products, body(): jnp.dot(hidden, w_down[0], preferred_element_type=jnp.float32)  20.6 us
    all_gather x1, blocking collectives, body(): lax.all_gather(attn_routes[0], 'exp', axis=0, tiled=True)  16.4 us
  transfers between devices with their start and end apart: 10, of which 6 were waited for; matrix products, arithmetic and copies ran while one was open for 22% of the time, Pallas kernels for 0%

commit v1 on v0

--- a/solution.py
+++ b/solution.py
@@ -8,6 +8,28 @@
 epsilon = 1e-05
 rope_base = 10000.0
 masked_score = -1e30
+
+
+def in_order(tiles, dim):
+    tiles = jnp.moveaxis(tiles, 0, dim)
+    shape = tiles.shape
+    return tiles.reshape(*shape[:dim], shape[dim] * shape[dim + 1], *shape[dim + 2 :])
+
+
+def gather_around(x, axis, dim):
+    devices = lax.axis_size(axis)
+    pairs = [(i, (i + 1) % devices) for i in range(devices)]
+    back = [(b, a) for a, b in pairs]
+    lower, upper = ([], [])
+    for turn in range(devices - 1):
+        if turn % 2 == 0:
+            lower.append(lax.ppermute(lower[-1] if lower else x, axis, pairs))
+        else:
+            upper.append(lax.ppermute(upper[-1] if upper else x, axis, back))
+    pieces = jnp.stack([*lower[::-1], x, *upper])
+    shift = lax.axis_index(axis) - len(lower)
+    pieces = pieces[(jnp.arange(devices) - shift) % devices]
+    return in_order(pieces, dim)
 
 
 def from_partner(value, axis, stride):
@@ -223,7 +245,7 @@
     split_count = device_count // experts_mlp
     my_expert = jnp.reshape(position // split_count, (1,))
     all_normed, all_routes = (
-        lax.all_gather(normed_mlp, "exp", axis=0, tiled=True),
+        gather_around(normed_mlp, "exp", 0),
         lax.all_gather(mlp_routes[0], "exp", axis=0, tiled=True),
     )
     all_gates = pick_gates(all_normed, mlp_router, all_routes)

time: 603 us -> 602 us (level)
  starting transfers between devices: 9.33 us -> 20.3 us
  waiting for transfers between devices: 320 us -> 310 us
    all_gather x1 -> x0, waiting for transfers between devices: 27.5 us -> none  [body(): lax.all_gather(normed_mlp, 'exp', axis=0, tiled=True)]
    ppermute x0 -> x7, waiting for transfers between devices: none -> 19.7 us  [the longest x4 19.5 us: gather_around(): lower.append(lax.ppermute(lower[-1] if lower else x, axis, pairs))]
    ppermute x0 -> x7, starting transfers between devices: none -> 11.2 us  [the longest x3 11.2 us: gather_around(): upper.append(lax.ppermute(upper[-1] if upper else x, axis, back))]
  transfers between devices with their start and end apart: 10 -> 16, of which waited for: 6 -> 10; matrix products, arithmetic and copies ran while one was open for 22% -> 23% of each run, Pallas kernels for 0% -> 0%
where the time goes in v1:
time: 602 us; the launch traced here: 597 us
  waiting for transfers between devices  310 us (51%)
  other arithmetic  76.9 us (13%)
  matrix products  73.4 us (12%)
  local copies, waits for them, and re-layouts  70.2 us (12%)
  blocking collectives  31.3 us (5%)
  starting transfers between devices  20.3 us (3%)
  between operations  15.2 us (3%)
    ppermute x6, waiting for transfers between devices, from_partner(): return lax.ppermute(value, axis, pairs)  231 us
    reduce_scatter x1, waiting for transfers between devices, body(): lax.psum_scatter(spread_rows(projected, attn_ids, rows_block * lax.axis_s...  35.9 us
    while x12, local copies, waits for them, and re-layouts  26.8 us
    select_n x5, other arithmetic, body(): jnp.where(lower, jnp.concatenate([group_cache, other_cache], axis=1), jnp...  25.2 us
    reduce_scatter x1, waiting for transfers between devices, body(): lax.psum_scatter(spread_rows(weighted, mlp_ids, rows_block * lax.axis_siz...  23.6 us
    dot_general x1, matrix products, body(): jnp.dot(hidden, w_down[0], preferred_element_type=jnp.float32)  20.5 us
    ppermute x4, waiting for transfers between devices, gather_around(): lower.append(lax.ppermute(lower[-1] if lower else x, axis, pairs))  19.5 us
    all_gather x1, blocking collectives, body(): lax.all_gather(attn_routes[0], 'exp', axis=0, tiled=True)  16.2 us
  transfers between devices with their start and end apart: 16, of which 10 were waited for; matrix products, arithmetic and copies ran while one was open for 23% of the time, Pallas kernels for 0%

profile of v1, /device:TPU:0, one launch (start us, length us, event | category | flops | bytes accessed | tf_op | source)
XLA Modules:
  0.0 597.5 jit_solution(13725021784859299663)
XLA Ops:
  14.0 16.2 %all-gather = s32[1,512,2]{2,0,1:T(1,128)S(1)} all-gather(s32[1,64,2]{2,0,1:T(1,128)S(1)} %copy.70), channel_id=2, replica_groups=mesh['req'=4,'exp'=8] {'exp'}, dimensions={1}, use_global_device_ids=true | all-gather | bytes 4608 | tf_op jit(solution)/shard_map/all_gather | solution.py:168
  30.4 15.1 %all-gather.1 = s32[1,512,2]{2,0,1:T(1,128)S(1)} all-gather(s32[1,64,2]{2,0,1:T(1,128)S(1)} %copy.88), channel_id=3, replica_groups=mesh['req'=4,'exp'=8] {'exp'}, dimensions={1}, use_global_device_ids=true | all-gather | bytes 4608 | tf_op jit(solution)/shard_map/all_gather | solution.py:249
  60.4 38.0 %collective-permute-done.1 = bf16[1024,1024]{1,0:T(8,128)(2,1)} collective-permute-done((bf16[1024,1024]{1,0:T(8,128)(2,1)}, bf16[1024,1024]{1,0:T(8,128)(2,1)}, u32[]{:S(2)}, u32[]{:S(2)}) %collective-permute-start.1) | collective-permute-done | bytes 2097184 | tf_op jit(solution)/shard_map/ppermute | solution.py:38
  98.4 6.7 %maximum_select_fusion.2 = bf16[1024,2048]{1,0:T(8,128)(2,1)} fusion(bf16[1024,1024]{1,0:T(8,128)(2,1)} %collective-permute-done.1, bf16[1024,1024]{1,0:T(8,128)(2,1)} %maximum_select_fusion.5, pred[]{:T(512)S(6)} %eq.116), kind=kLoop, calls=%fused_computation.45 | loop fusion | flops 18874368 | bytes 8388609 | tf_op jit(solution)/shard_map/jit(_where)/select_n | solution.py:200
  111.5 5.1 maximum_select_fusion.1
  127.9 5.2 convolution_bitcast_fusion.1
  135.6 84.5 %collective-permute-done.4 = bf16[512,1024]{0,1:T(8,128)(2,1)S(1)} collective-permute-done((bf16[512,1024]{0,1:T(8,128)(2,1)S(1)}, bf16[512,1024]{0,1:T(8,128)(2,1)S(1)}, u32[]{:S(2)}, u32[]{:S(2)}) %collective-permute-start.4) | collective-permute-done | bytes 1048608 | tf_op jit(solution)/shard_map/ppermute | solution.py:38
  226.3 108.2 %collective-permute-done.2 = bf16[1024,2048]{1,0:T(8,128)(2,1)} collective-permute-done((bf16[1024,2048]{1,0:T(8,128)(2,1)}, bf16[1024,2048]{1,0:T(8,128)(2,1)}, u32[]{:S(2)}, u32[]{:S(2)}) %collective-permute-start.2) | collective-permute-done | bytes 4194336 | tf_op jit(solution)/shard_map/ppermute | solution.py:38
  334.5 6.4 %copy.75 = bf16[1024,2048]{0,1:T(8,128)(2,1)} copy(bf16[1024,2048]{1,0:T(8,128)(2,1)} %collective-permute-done.2) | data formatting | bytes 8388608 | tf_op jit(solution)/shard_map/ppermute | solution.py:38
  340.9 6.6 %maximum_select_fusion = bf16[1024,16,2,128]{0,3,2,1:T(8,128)(2,1)S(1)} fusion(bf16[1024,8,2,128]{0,3,2,1:T(8,128)(2,1)} %bitcast.181, bf16[1024,8,2,128]{0,3,2,1:T(8,128)(2,1)} %maximum_select_fusion.1, pred[]{:T(512)S(6)} %eq.115), kind=kLoop, calls=%fused_computation.34 | loop fusion | flops 12582912 | bytes 16777216 | tf_op jit(solution)/shard_map/jit(_where)/select_n | solution.py:200
  352.6 51.5 %while.16 = (s32[]{:T(128)}, f32[16,192]{1,0:T(8,128)S(1)}, f32[16,192]{1,0:T(8,128)S(1)}, f32[16,192,128]{2,1,0:T(8,128)}, s32[]{:T(128)}, /*index=5*/s32[]{:T(...) while((s32[]{:T(128)}, f32[16,192]{1,0:T(8,128)S(1)}, ...), condition=%wide.region_7.8_spmd, body=%wide.region_4.7_spmd.sunk | while | flops 823401472 | bytes 69142768 | solution.py:127
  353.3 6.4 %constant_dynamic-slice_fusion.3 = (bf16[512,16,128]{0,2,1:T(8,128)(2,1)S(1)}, bf16[512,16,128]{0,2,1:T(8,128)(2,1)}) fusion(bf16[1024,16,128]{0,2,1:T(8,128)(2,1)} %get-tuple-element.252, s32[]{:T(128)S(1)} %bitcast.196, bf16[1024,16,128]{0,2,1:T(8,128)(2,1)} %get-tuple-element.250), kind=kLoop, calls=%fused_computation.24.clone.1 | loop fusion | bytes 8388612 | tf_op jit(solution)/shard_map/vmap()/while
  371.4 6.9 %multiply_add_fusion.7 = f32[16,192,128]{2,1,0:T(8,128)} fusion(f32[16,192,128]{2,1,0:T(8,128)} %get-tuple-element.233, bf16[512,16,128]{2,0,1:T(8,128)(2,1)} %copy.105, f32[16,512,192]{1,2,0:T(8,128)} %copy-done.2, f32[16,192]{1,0:T(8,128)S(1)} %max.10, pred[512]{0:T(512)(128)(4,1)S(1)} %add_compare_fusion.2, f32[16,192]{1,0:T(8,128)S(1)} %get-tuple-element.215), kind=kOutput, calls=%fused_computation.19.clone.1 | convolution fusion | flops 409731072 | bytes 11559424 | tf_op jit(solution)/shard_map/vmap()/while/body/dot_general | solution.py:108
  379.1 6.1 %constant_dynamic-slice_fusion.3 = (bf16[512,16,128]{0,2,1:T(8,128)(2,1)S(1)}, bf16[512,16,128]{0,2,1:T(8,128)(2,1)}) fusion(bf16[1024,16,128]{0,2,1:T(8,128)(2,1)} %get-tuple-element.252, s32[]{:T(128)S(1)} %bitcast.196, bf16[1024,16,128]{0,2,1:T(8,128)(2,1)} %get-tuple-element.250), kind=kLoop, calls=%fused_computation.24.clone.1 | loop fusion | bytes 8388612 | tf_op jit(solution)/shard_map/vmap()/while
  396.9 6.9 %multiply_add_fusion.7 = f32[16,192,128]{2,1,0:T(8,128)} fusion(f32[16,192,128]{2,1,0:T(8,128)} %get-tuple-element.233, bf16[512,16,128]{2,0,1:T(8,128)(2,1)} %copy.105, f32[16,512,192]{1,2,0:T(8,128)} %copy-done.2, f32[16,192]{1,0:T(8,128)S(1)} %max.10, pred[512]{0:T(512)(128)(4,1)S(1)} %add_compare_fusion.2, f32[16,192]{1,0:T(8,128)S(1)} %get-tuple-element.215), kind=kOutput, calls=%fused_computation.19.clone.1 | convolution fusion | flops 409731072 | bytes 11559424 | tf_op jit(solution)/shard_map/vmap()/while/body/dot_general | solution.py:108
  413.1 10.8 %fusion.39 = f32[192,2048]{1,0:T(8,128)} fusion(bf16[16,128,2048]{2,1,0:T(8,128)(2,1)} %param.26, f32[16,192,128]{2,1,0:T(8,128)S(1)} %copy-done.12, bf16[512,16,2,128]{0,3,1,2:T(8,128)(2,1)} %copy-done.7, f32[16,192,512]{2,1,0:T(8,128)} %copy-done.4, f32[16,192]{1,0:T(8,128)S(1)} %max.8, pred[192,512]{1,0:T(8,128)(4,1)S(1)} %iota_compare_fusion, ...), kind=kOutput, calls=%fused_computation.53 | convolution fusion | flops 2021523456 | bytes 20058880 | tf_op jit(solution)/shard_map/hsk,hkd->sd/dot_general | solution.py:231
  423.8 5.9 scatter_custom_fusion
  433.7 35.9 %reduce-scatter.3.cloned.1.call-done = bf16[64,2048]{1,0:T(8,128)(2,1)} async-done(((bf16[512,2048]{1,0:T(8,128)(2,1)}), bf16[64,2048]{1,0:T(8,128)(2,1)}) %reduce-scatter.3.cloned.1.call-update) | async-done | bytes 262160 | tf_op jit(solution)/shard_map/reduce_scatter | solution.py:234
  471.0 7.8 %collective-permute-done.6 = bf16[64,2048]{1,0:T(8,128)(2,1)S(1)} collective-permute-done((bf16[64,2048]{1,0:T(8,128)(2,1)S(1)}, bf16[64,2048]{1,0:T(8,128)(2,1)S(1)}, u32[]{:S(2)}, u32[]{:S(2)}) %collective-permute-start.6) | collective-permute-done | bytes 262176 | tf_op jit(solution)/shard_map/ppermute | solution.py:26
  512.1 12.0 %fusion.22 = f32[192,5632]{1,0:T(8,128)} fusion(bf16[192,2048]{1,0:T(8,128)(2,1)S(1)} %gather_fusion.2, bf16[1,2048,5632]{2,1,0:T(8,128)(2,1)} %param.29), kind=kOutput, calls=%fused_computation.32 | convolution fusion | flops 4429185024 | bytes 28180480 | tf_op jit(solution)/shard_map/dot_general | solution.py:254
  524.1 20.5 %fusion.40 = bf16[192,2048]{1,0:T(8,128)(2,1)S(1)} fusion(bf16[1,5632,2048]{2,1,0:T(8,128)(2,1)} %param.31, bf16[192,2048]{1,0:T(8,128)(2,1)} %copy-done.14, bf16[1,2048,5632]{2,1,0:T(8,128)(2,1)} %param.30, f32[192,5632]{1,0:T(8,128)} %fusion.22), kind=kOutput, calls=%fused_computation.54 | convolution fusion | flops 8865251328 | bytes 52035584 | tf_op jit(solution)/shard_map/dot_general | solution.py:258
  545.7 5.2 scatter_custom_fusion.1
  558.0 4.3 dynamic_update_slice.3
  565.4 23.6 %reduce-scatter.5.cloned.1.call-done = bf16[64,2048]{1,0:T(8,128)(2,1)} async-done(((bf16[512,2048]{1,0:T(8,128)(2,1)}), bf16[64,2048]{1,0:T(8,128)(2,1)}) %reduce-scatter.5.cloned.1.call-update) | async-done | bytes 262160 | tf_op jit(solution)/shard_map/reduce_scatter | solution.py:264
  (208 shorter events, 137.5 us)
Async XLA Ops:
  7.2 109.4 %copy-start = (bf16[2048,512]{1,0:T(8,128)(2,1)S(1)}, bf16[2048,512]{1,0:T(8,128)(2,1)}, u32[]{:S(2)}) copy-start(bf16[2048,512]{1,0:T(8,128)(2,1)} %param.25) | copy-start | bytes 6291460
  7.2 23.1 %copy-start.27 = (s32[1,64,2]{1,2,0:T(2,128)S(1)}, s32[1,64,2]{1,2,0:T(2,128)}, u32[]{:S(2)}) copy-start(s32[1,64,2]{1,2,0:T(2,128)} %param.21) | copy-start | bytes 1540
  7.2 109.4 %all-gather.4.cloned.1.call-start = ((), (), s32[]{:S(2)}) async-start(), calls=%async_computation.2 | async-start | bytes 2359296 | tf_op jit(solution)/shard_map/all_gather | solution.py:167
  7.2 39.4 %collective-permute-start = (bf16[1024,512]{1,0:T(8,128)(2,1)}, bf16[1024,512]{1,0:T(8,128)(2,1)}, u32[]{:S(2)}, u32[]{:S(2)}) collective-permute-start(bf16[1024,512]{1,0:T(8,128)(2,1)} %bitcast.182), channel_id=1, source_target_pairs={{0,1},{1,0},{2,3},{3,2},{4,5},{5,4},{6,7},{7,6},{8,9},{9,8},{10,11... | collective-permute-start | bytes 3145736 | tf_op jit(solution)/shard_map/ppermute | solution.py:38
  8.9 37.7 %copy-start.5 = (bf16[1,1024,512]{2,1,0:T(8,128)(2,1)S(1)}, bf16[1,1024,512]{2,1,0:T(8,128)(2,1)}, u32[]{:S(2)}) copy-start(bf16[1,1024,512]{2,1,0:T(8,128)(2,1)} %param.18) | copy-start | bytes 3145732
  10.9 458.8 %reduce-scatter.3.cloned.1.call-start = ((), (), s32[]{:S(2)}) async-start(), calls=%async_computation.3 | async-start | bytes 2359296 | tf_op jit(solution)/shard_map/reduce_scatter | solution.py:234
  50.2 48.2 %collective-permute-start.1 = (bf16[1024,1024]{1,0:T(8,128)(2,1)}, bf16[1024,1024]{1,0:T(8,128)(2,1)}, u32[]{:S(2)}, u32[]{:S(2)}) collective-permute-start(bf16[1024,1024]{1,0:T(8,128)(2,1)} %maximum_select_fusion.5), channel_id=1, source_target_pairs={{0,2},{1,3},{2,0},{3,1},{4,6},{5,7},{6,4},{7,5},{8,10},{9,11},{10,... | collective-permute-start | bytes 6291464 | tf_op jit(solution)/shard_map/ppermute | solution.py:38
  105.2 229.4 %collective-permute-start.2 = (bf16[1024,2048]{1,0:T(8,128)(2,1)}, bf16[1024,2048]{1,0:T(8,128)(2,1)}, u32[]{:S(2)}, u32[]{:S(2)}) collective-permute-start(bf16[1024,2048]{1,0:T(8,128)(2,1)} %maximum_select_fusion.2), channel_id=1, source_target_pairs={{0,4},{1,5},{2,6},{3,7},{4,0},{5,1},{6,2},{7,3},{8,12},{9,13},{10,... | collective-permute-start | bytes 12582920 | tf_op jit(solution)/shard_map/ppermute | solution.py:38
  119.8 4.6 collective-permute-start.3
  126.1 94.1 %collective-permute-start.4 = (bf16[512,1024]{0,1:T(8,128)(2,1)S(1)}, bf16[512,1024]{0,1:T(8,128)(2,1)S(1)}, u32[]{:S(2)}, u32[]{:S(2)}) collective-permute-start(bf16[512,1024]{0,1:T(8,128)(2,1)S(1)} %maximum_select_fusion.9), channel_id=1, source_target_pairs={{0,2},{1,3},{2,0},{3,1},{4,6},{5,7},{6,4},{7,5},{8,10},{9,11},{10,... | collective-permute-start | bytes 3145736 | tf_op jit(solution)/shard_map/ppermute | solution.py:38
  222.2 181.9 %collective-permute-start.5 = (bf16[512,2048]{0,1:T(8,128)(2,1)}, bf16[512,2048]{0,1:T(8,128)(2,1)}, u32[]{:S(2)}, u32[]{:S(2)}) collective-permute-start(bf16[512,2048]{0,1:T(8,128)(2,1)} %maximum_select_fusion.7), channel_id=1, source_target_pairs={{0,4},{1,5},{2,6},{3,7},{4,0},{5,1},{6,2},{7,3},{8,12},{9,13},{10,... | collective-permute-start | bytes 6291464 | tf_op jit(solution)/shard_map/ppermute | solution.py:38
  433.6 36.0 %copy-start.11 = (bf16[1,64,2048]{2,1,0:T(8,128)(2,1)S(1)}, bf16[1,64,2048]{2,1,0:T(8,128)(2,1)}, u32[]{:S(2)}) copy-start(bf16[1,64,2048]{2,1,0:T(8,128)(2,1)} %param.17) | copy-start | bytes 786436
  433.6 37.2 %copy-start.23 = (f32[2048]{0:T(1024)S(1)}, f32[2048]{0:T(1024)}, u32[]{:S(2)}) copy-start(f32[2048]{0:T(1024)} %param.27) | copy-start | bytes 24580
  433.6 155.3 %reduce-scatter.5.cloned.1.call-start = ((), (), s32[]{:S(2)}) async-start(), calls=%async_computation.4 | async-start | bytes 2359296 | tf_op jit(solution)/shard_map/reduce_scatter | solution.py:264
  470.9 7.8 %collective-permute-start.6 = (bf16[64,2048]{1,0:T(8,128)(2,1)S(1)}, bf16[64,2048]{1,0:T(8,128)(2,1)S(1)}, u32[]{:S(2)}, u32[]{:S(2)}) collective-permute-start(bf16[64,2048]{1,0:T(8,128)(2,1)S(1)} %fusion.62), channel_id=1, source_target_pairs={{0,1},{1,2},{2,3},{3,4},{4,5},{5,6},{6,7},{7,0},{8,9},{9,10},{10,1... | collective-permute-start | bytes 786440 | tf_op jit(solution)/shard_map/ppermute | solution.py:26
  478.8 7.8 %collective-permute-start.7 = (bf16[64,2048]{1,0:T(8,128)(2,1)S(1)}, bf16[64,2048]{1,0:T(8,128)(2,1)S(1)}, u32[]{:S(2)}, u32[]{:S(2)}) collective-permute-start(bf16[64,2048]{1,0:T(8,128)(2,1)S(1)} %collective-permute-done.6), channel_id=1, source_target_pairs={{0,1},{1,2},{2,3},{3,4},{4,5},{5,6},{6,7},{7,0},{8,9},{9,10},{10,1... | collective-permute-start | bytes 786440 | tf_op jit(solution)/shard_map/ppermute | solution.py:26
  478.8 7.9 %collective-permute-start.10 = (bf16[64,2048]{1,0:T(8,128)(2,1)S(1)}, bf16[64,2048]{1,0:T(8,128)(2,1)S(1)}, u32[]{:S(2)}, u32[]{:S(2)}) collective-permute-start(bf16[64,2048]{1,0:T(8,128)(2,1)S(1)} %fusion.62), channel_id=1, source_target_pairs={{1,0},{2,1},{3,2},{4,3},{5,4},{6,5},{7,6},{0,7},{9,8},{10,9},{11,1... | collective-permute-start | bytes 786440 | tf_op jit(solution)/shard_map/ppermute | solution.py:28
  486.5 7.8 %collective-permute-start.8 = (bf16[64,2048]{1,0:T(8,128)(2,1)S(1)}, bf16[64,2048]{1,0:T(8,128)(2,1)S(1)}, u32[]{:S(2)}, u32[]{:S(2)}) collective-permute-start(bf16[64,2048]{1,0:T(8,128)(2,1)S(1)} %collective-permute-done.7), channel_id=1, source_target_pairs={{0,1},{1,2},{2,3},{3,4},{4,5},{5,6},{6,7},{7,0},{8,9},{9,10},{10,1... | collective-permute-start | bytes 786440 | tf_op jit(solution)/shard_map/ppermute | solution.py:26
  486.6 7.7 %collective-permute-start.11 = (bf16[64,2048]{1,0:T(8,128)(2,1)S(1)}, bf16[64,2048]{1,0:T(8,128)(2,1)S(1)}, u32[]{:S(2)}, u32[]{:S(2)}) collective-permute-start(bf16[64,2048]{1,0:T(8,128)(2,1)S(1)} %collective-permute-done.10), channel_id=1, source_target_pairs={{1,0},{2,1},{3,2},{4,3},{5,4},{6,5},{7,6},{0,7},{9,8},{10,9},{11,1... | collective-permute-start | bytes 786440 | tf_op jit(solution)/shard_map/ppermute | solution.py:28
  494.3 7.6 %collective-permute-start.9 = (bf16[64,2048]{1,0:T(8,128)(2,1)S(1)}, bf16[64,2048]{1,0:T(8,128)(2,1)S(1)}, u32[]{:S(2)}, u32[]{:S(2)}) collective-permute-start(bf16[64,2048]{1,0:T(8,128)(2,1)S(1)} %collective-permute-done.8), channel_id=1, source_target_pairs={{0,1},{1,2},{2,3},{3,4},{4,5},{5,6},{6,7},{7,0},{8,9},{9,10},{10,1... | collective-permute-start | bytes 786440 | tf_op jit(solution)/shard_map/ppermute | solution.py:26
  494.3 12.7 %collective-permute-start.12 = (bf16[64,2048]{1,0:T(8,128)(2,1)S(1)}, bf16[64,2048]{1,0:T(8,128)(2,1)S(1)}, u32[]{:S(2)}, u32[]{:S(2)}) collective-permute-start(bf16[64,2048]{1,0:T(8,128)(2,1)S(1)} %collective-permute-done.11), channel_id=1, source_target_pairs={{1,0},{2,1},{3,2},{4,3},{5,4},{6,5},{7,6},{0,7},{9,8},{10,9},{11,1... | collective-permute-start | bytes 786440 | tf_op jit(solution)/shard_map/ppermute | solution.py:28
  524.0 20.5 %copy-start.22 = (bf16[2048,8]{0,1:T(8,128)(2,1)S(1)}, bf16[2048,8]{0,1:T(8,128)(2,1)}, u32[]{:S(2)}) copy-start(bf16[2048,8]{0,1:T(8,128)(2,1)} %param.28) | copy-start | bytes 98308
  554.8 7.6 %copy-start.6 = (bf16[1,1024,512]{2,1,0:T(8,128)(2,1)S(1)}, bf16[1,1024,512]{2,1,0:T(8,128)(2,1)}, u32[]{:S(2)}) copy-start(bf16[1,1024,512]{2,1,0:T(8,128)(2,1)} %param.18) | copy-start | bytes 3145732
  558.0 32.7 %copy-start.1 = (bf16[2048,512]{1,0:T(8,128)(2,1)S(1)}, bf16[2048,512]{1,0:T(8,128)(2,1)}, u32[]{:S(2)}) copy-start(bf16[2048,512]{1,0:T(8,128)(2,1)} %param.25) | copy-start | bytes 6291460
  (21 other events, 67.1 us)
Sparse Core Ops, SparseCore 0:
  11.0 34.2 all-gather.3
  433.8 35.7 reduce-scatter.2
  554.9 34.0 reduce-scatter.4
